TPU v7x, 128 devices: a whole 4x4x4 slice. The times are simulated.
128 devices in a mesh: req: 64 (over z, y, x), blk: 2 (over core).
Axes of the slice: x: 4, y: 4, z: 4, core: 2. Of those that a mesh axis runs over, the one named last changes fastest.
Arguments:
- normed: bfloat16 [32768, 1536], P('req', 'blk'), may hold values from -6 to 6
- router: bfloat16 [1536, 64], P('blk'), may hold values from -0.15625 to 0.15625
- adapter_down: bfloat16 [1536, 256], P('blk'), may hold values from -0.15625 to 0.15625
- adapter_up: bfloat16 [256, 1536], P(None, 'blk'), may hold values from -1.5 to 1.5
- shared_gate_up: bfloat16 [1536, 2, 1024], P(None, None, 'blk'), may hold values from -0.15625 to 0.15625
- shared_down: bfloat16 [1024, 1536], P('blk'), may hold values from -0.1875 to 0.1875
- expert_gate_up: bfloat16 [64, 1536, 1024], P('req', 'blk'), may hold values from -0.15625 to 0.15625
- expert_down: bfloat16 [64, 512, 1536], P('req', None, 'blk'), may hold values from -0.25 to 0.25
- lengths: int32 [64, 4], P('req'), may hold values from 1 to 256, 512 in all within a row
- adapter_ids: int32 [64, 4], P('req'), may hold values from 0 to 15
- routes: int32 [32768, 6], P('req'), may hold values from 0 to 63, all different within a row; in each aligned block of 512 rows (0 to 511, 512 to 1023, ...) at most 52 rows name the same one
Outputs:
- mixed: bfloat16 [32768, 1536], P('req', 'blk')
Inputs may be any that keep to these rules, and one draw needn't show every extreme that they name: `lengths`: each row of an index of req lists its 4 prompts in token order; they sum to 512, the longest is 256. `routes`: each row names 6 different experts. Among the 512 rows of one index of req no expert is named more than 52 times, a bound that some block reaches.
All inputs are finite; a program needn't handle non-finite values.
Results may differ from a plain program's by a relative error of at most 0.013.
Values may be sent and summed in bfloat16 or wider, within the bound.
No kernel may reach another device: no remote copies, remote signals or barrier semaphores. Data moves between devices by JAX's collectives and lax.ppermute only.
A program may use at most 128 MiB of HBM per device.

v0:
```python
import jax
import jax.numpy as jnp
from jax import lax
from jax.sharding import PartitionSpec as P

RANK = 16


def slot_table(target, source_row, total_slots):
    source_slot = jnp.zeros((total_slots,), jnp.int32).at[target].set(source_row)
    filled = jnp.zeros((total_slots,), jnp.int32).at[target].set(1)
    return (source_slot, filled)


def body(
    normed,
    router,
    adapter_down,
    adapter_up,
    shared_gate_up,
    shared_down,
    expert_gate_up,
    expert_down,
    lengths,
    adapter_ids,
    routes,
):
    tok_rows = normed.shape[0]
    feat_local = normed.shape[1]
    top_count = routes.shape[1]
    req_count = lax.axis_size("req")
    expert_count = req_count * expert_gate_up.shape[0]
    most_rows = (
        tok_rows * top_count + expert_count - 1
    ) // expert_count + tok_rows * top_count // (12 * expert_count)
    slot_count = req_count * most_rows
    hidden_width = expert_down.shape[1]
    logit_part = jnp.dot(normed, router, preferred_element_type=jnp.float32)
    low_part = jnp.dot(normed, adapter_down, preferred_element_type=jnp.float32)
    logits, low_all = (
        lax.psum(logit_part.astype(jnp.bfloat16), "blk").astype(jnp.float32),
        lax.psum(low_part.astype(jnp.bfloat16), "blk").astype(jnp.float32),
    )
    ends = jnp.cumsum(lengths[0])
    position = jnp.arange(tok_rows, dtype=jnp.int32)
    request = jnp.sum((position[:, None] >= ends[None, :]).astype(jnp.int32), axis=1)
    slots_req = jnp.arange(lengths.shape[1], dtype=jnp.int32)
    adapter_token = jnp.sum(
        jnp.where(request[:, None] == slots_req[None, :], adapter_ids[0][None, :], 0), axis=1
    )
    column_owner = jnp.arange(low_all.shape[1], dtype=jnp.int32) // RANK
    low = jnp.where(column_owner[None, :] == adapter_token[:, None], low_all, 0.0).astype(
        jnp.bfloat16
    )
    delta = jnp.dot(low, adapter_up, preferred_element_type=jnp.float32)
    shared_local = shared_gate_up.shape[2]
    shared_flat = shared_gate_up.reshape(shared_gate_up.shape[0], 2 * shared_local)
    shared_pre = jnp.dot(
        lax.all_gather(normed, "blk", axis=1, tiled=True),
        shared_flat,
        preferred_element_type=jnp.float32,
    )
    shared_hidden = (
        jax.nn.silu(shared_pre[:, :shared_local]) * shared_pre[:, shared_local:]
    ).astype(jnp.bfloat16)
    shared_terms = jnp.dot(shared_hidden, shared_down, preferred_element_type=jnp.float32)
    shared_out = lax.psum_scatter(
        shared_terms.astype(jnp.bfloat16), "blk", scatter_dimension=1, tiled=True
    ).astype(jnp.float32)
    scores = jax.nn.sigmoid(logits)
    chosen = jnp.take_along_axis(scores, routes, axis=1)
    gate_weight = chosen / jnp.sum(chosen, axis=1, keepdims=True)
    flat_expert = routes.reshape(-1)
    one_hot = (flat_expert[:, None] == jnp.arange(expert_count, dtype=jnp.int32)[None, :]).astype(
        jnp.int32
    )
    earlier = jnp.cumsum(one_hot, axis=0) - one_hot
    slot_rank = jnp.sum(earlier * one_hot, axis=1)
    source_row = jnp.arange(tok_rows * top_count, dtype=jnp.int32) // top_count
    weight_gate_up = expert_gate_up[0]
    weight_down = expert_down[0]
    target = flat_expert * most_rows + slot_rank
    source_slot, filled = slot_table(target, source_row, expert_count * most_rows)
    send_rows = jnp.where(filled[:, None] > 0, normed[source_slot], jnp.zeros((), jnp.bfloat16))
    received = lax.all_to_all(
        send_rows.reshape(expert_count, most_rows, feat_local),
        "req",
        split_axis=0,
        concat_axis=0,
        tiled=True,
    )
    rows_in = received.reshape(slot_count, feat_local)
    gate_up = lax.psum_scatter(
        jnp.dot(rows_in, weight_gate_up, preferred_element_type=jnp.float32).astype(jnp.bfloat16),
        "blk",
        scatter_dimension=0,
        tiled=True,
    ).astype(jnp.float32)
    hidden = (jax.nn.silu(gate_up[:, :hidden_width]) * gate_up[:, hidden_width:]).astype(
        jnp.bfloat16
    )
    expert_out = jnp.dot(
        lax.all_gather(hidden, "blk", axis=0, tiled=True),
        weight_down,
        preferred_element_type=jnp.float32,
    ).astype(jnp.bfloat16)
    returned = lax.all_to_all(
        expert_out.reshape(req_count, most_rows, feat_local),
        "req",
        split_axis=0,
        concat_axis=0,
        tiled=True,
    )
    picked = returned.reshape(expert_count * most_rows, feat_local)[target].astype(jnp.float32)
    weighted = picked * gate_weight.reshape(-1)[:, None]
    routed = jnp.sum(weighted.reshape(tok_rows, top_count, feat_local), axis=1)
    return (shared_out + 0.5 * delta + routed).astype(jnp.bfloat16)


def solution(mesh):
    return jax.shard_map(
        body,
        mesh=mesh,
        in_specs=(
            P("req", "blk"),
            P("blk", None),
            P("blk", None),
            P(None, "blk"),
            P(None, None, "blk"),
            P("blk", None),
            P("req", "blk", None),
            P("req", None, "blk"),
            P("req", None),
            P("req", None),
            P("req", None),
        ),
        out_specs=P("req", "blk"),
        check_vma=False,
    )
```

profile of v0, /device:TPU:10, one launch (start us, length us, event | category | flops | bytes accessed | tf_op | source)
XLA Modules:
  0.0 384.7 jit_solution(10369042271794032363)
XLA Ops:
  9.5 32.0 %reduce-window.19 = s32[64,24,128]{2,1,0:T(8,128)S(1)} reduce-window(s32[64,24,128]{2,1,0:T(8,128)} %fusion.7, s32[]{:T(128)} %constant.58.clone.1), window={size=1x1x128 pad=0_0x0_0x127_0}, to_apply=%region_5.6 | reduce-window | flops 24969216 | bytes 1572868 | tf_op jit(solution)/shard_map/reduce-window.1
  41.5 1.2 slice.32
  42.7 1.6 copy.41
  44.4 1.2 broadcast_add_fusion
  45.9 1.3 fusion.5
  47.3 11.8 %scatter_custom_fusion.1 = s32[3328]{0:T(1024)S(1)} fusion(s32[3072]{0:T(1024)S(1)} %bitcast.52, s32[3072]{0:T(1024)S(1)} %add_select_fusion, s32[]{:T(128)} %constant.58.clone.1), kind=kCustom, calls=%fused_computation.48 | custom fusion | bytes 13316 | tf_op jit(solution)/shard_map/scatter | solution.py:10
  59.1 10.8 %gather_fusion = bf16[3328,768]{1,0:T(8,128)(2,1)} fusion(bf16[512,768]{1,0:T(8,128)(2,1)S(1)} %copy-done.2, s32[4096]{0:T(1024)S(1)} %pad_clamp_fusion), kind=kCustom, calls=%fused_computation | custom fusion | bytes 10236928 | tf_op jit(solution)/shard_map/gather | solution.py:84
  70.0 7.4 %gather.13 = bf16[64,52,768]{2,1,0:T(8,128)(2,1)} reshape(bf16[3328,768]{1,0:T(8,128)(2,1)} %gather_fusion) | data formatting | bytes 10223616 | tf_op jit(solution)/shard_map/gather | solution.py:84
  77.3 11.8 %scatter_custom_fusion = s32[3328]{0:T(1024)S(1)} fusion(s32[3072]{0:T(1024)S(1)} %bitcast.53, s32[3072]{0:T(1024)S(1)} %broadcast.128, s32[]{:T(128)} %constant.58.clone.1), kind=kCustom, calls=%fused_computation.51 | custom fusion | bytes 13316 | tf_op jit(solution)/shard_map/scatter | solution.py:11
  89.3 3.6 broadcast_select_fusion
  92.9 76.0 %all_to_all.10 = bf16[64,52,768]{2,1,0:T(8,128)(2,1)} all-to-all(bf16[64,52,768]{2,1,0:T(8,128)(2,1)S(1)} %broadcast_select_fusion), channel_id=1, replica_groups=mesh['req'=64,'blk'=2] {'req'}, dimensions={0} | all-to-all | bytes 10223616 | tf_op jit(solution)/shard_map/all_to_all | solution.py:85
  168.9 7.4 %reshape.143 = bf16[3328,768]{1,0:T(8,128)(2,1)} reshape(bf16[64,52,768]{2,1,0:T(8,128)(2,1)} %all_to_all.10) | data formatting | bytes 10223616 | tf_op jit(solution)/shard_map/reshape | solution.py:92
  176.3 10.0 %convolution_convert_fusion = bf16[3328,1024]{1,0:T(8,128)(2,1)} fusion(bf16[3328,768]{1,0:T(8,128)(2,1)} %reshape.143, bf16[1,768,1024]{2,1,0:T(8,128)(2,1)S(1)} %copy-done), kind=kOutput, calls=%fused_computation.6 | convolution fusion | flops 5237899264 | bytes 13500416 | tf_op jit(solution)/shard_map/dot_general | solution.py:94
  186.5 16.7 %reduce-scatter.5.cloned.1.call-done = bf16[1664,1024]{1,0:T(8,128)(2,1)} async-done(((bf16[3328,1024]{1,0:T(8,128)(2,1)}), bf16[1664,1024]{1,0:T(8,128)(2,1)}) %reduce-scatter.5.cloned.1.call-update) | async-done | bytes 3407888 | tf_op jit(solution)/shard_map/reduce_scatter | solution.py:93
  203.2 2.8 convert_element_type.66
  206.0 2.4 fusion
  208.4 16.7 %all-gather.5.cloned.1.call-done = bf16[3328,512]{1,0:T(8,128)(2,1)} async-done(((bf16[1664,512]{1,0:T(8,128)(2,1)}), bf16[3328,512]{1,0:T(8,128)(2,1)}) %all-gather.5.cloned.1.call-update) | async-done | bytes 3407888 | tf_op jit(solution)/shard_map/all_gather | solution.py:103
  225.1 7.0 %convolution_convert_fusion.1 = bf16[3328,768]{1,0:T(8,128)(2,1)} fusion(bf16[3328,512]{1,0:T(8,128)(2,1)} %all-gather.5.cloned.1.call-done, bf16[1,512,768]{2,1,0:T(8,128)(2,1)S(1)} %copy-done.9), kind=kOutput, calls=%fused_computation.7 | convolution fusion | flops 2619801600 | bytes 9306112 | tf_op jit(solution)/shard_map/dot_general | solution.py:102
  232.2 7.4 %reshape.144 = bf16[64,52,768]{2,1,0:T(8,128)(2,1)} reshape(bf16[3328,768]{1,0:T(8,128)(2,1)} %convolution_convert_fusion.1) | data formatting | bytes 10223616 | tf_op jit(solution)/shard_map/reshape | solution.py:108
  239.6 10.7 %all-to-all-start.1 = ((bf16[64,52,768]{2,1,0:T(8,128)(2,1)}), bf16[64,52,768]{2,1,0:T(8,128)(2,1)}, u32[]{:S(2)}, u32[]{:S(2)}) async-start(bf16[64,52,768]{2,1,0:T(8,128)(2,1)} %reshape.144), calls=%async_computation.3 | async-start | bytes 11010048 | tf_op jit(solution)/shard_map/all_to_all | solution.py:107
  253.5 4.5 %copy.42 = bf16[192,8,2,512]{3,1,2,0:T(8,128)(2,1)} copy(bf16[192,8,2,512]{3,2,1,0:T(2,128)(2,1)} %bitcast.47) | data formatting | bytes 6291456
  257.9 8.6 %all-gather.3.cloned.1.call-done = bf16[512,1536]{1,0:T(8,128)(2,1)} async-done(((bf16[512,768]{1,0:T(8,128)(2,1)}), bf16[512,1536]{1,0:T(8,128)(2,1)}) %all-gather.3.cloned.1.call-update) | async-done | bytes 1572880 | tf_op jit(solution)/shard_map/all_gather | solution.py:59
  266.6 4.3 %fusion.23 = f32[512,1024]{1,0:T(8,128)S(1)} fusion(bf16[512,1536]{1,0:T(8,128)(2,1)} %all-gather.3.cloned.1.call-done, bf16[1536,1024]{1,0:T(8,128)(2,1)} %bitcast.48), kind=kOutput, calls=%fused_computation.65 | convolution fusion | flops 1610612736 | bytes 6815744 | tf_op jit(solution)/shard_map/dot_general | solution.py:58
  270.9 2.2 convolution_convert_fusion.2
  273.9 20.4 %all-reduce.3.cloned.1.call-done = (bf16[512,64]{0,1:T(8,128)(2,1)}, bf16[512,256]{1,0:T(8,128)(2,1)}) async-done(((bf16[512,64]{0,1:T(8,128)(2,1)}, bf16[512,256]{1,0:T(8,128)(2,1)}), (bf16[512,64]{0,1:T(8,128)(2,1)}, bf16[512,256]{1,0:T(8,128)(2,1)})) %all-reduce.3.cloned.1.call-update) | async-done | bytes 327696 | tf_op jit(solution)/shard_map/psum | solution.py:41
  295.2 24.9 %gather_fusion.2 = f32[3072]{0:T(1024)S(1)} fusion(f32[512,64]{0,1:T(8,128)S(1)} %add_divide_fusion, s32[3072]{0:T(1024)S(1)} %reshape.164), kind=kCustom, calls=%fused_computation.2 | custom fusion | bytes 49152 | tf_op jit(solution)/shard_map/jit(take_along_axis)/gather | solution.py:71
  320.6 3.3 all-to-all-done.1
  324.0 7.4 %reshape.145 = bf16[3328,768]{1,0:T(8,128)(2,1)} reshape(bf16[64,52,768]{2,1,0:T(8,128)(2,1)} %all-to-all-done.1) | data formatting | bytes 10223616 | tf_op jit(solution)/shard_map/reshape | solution.py:114
  331.4 17.7 %gather_fusion.1 = bf16[3072,768]{1,0:T(8,128)(2,1)} fusion(bf16[3328,768]{1,0:T(8,128)(2,1)} %reshape.145, s32[3072]{0:T(1024)S(1)} %broadcast_clamp_fusion), kind=kCustom, calls=%fused_computation.1 | custom fusion | bytes 9449472 | tf_op jit(solution)/shard_map/gather | solution.py:114
  349.1 9.2 %reshape.147 = f32[512,6,768]{2,1,0:T(8,128)} reshape(bf16[3072,768]{1,0:T(8,128)(2,1)} %gather_fusion.1) | data formatting | bytes 14155776 | tf_op jit(solution)/shard_map/convert_element_type | solution.py:114
  358.2 17.2 %multiply_reduce_fusion = f32[512,768]{1,0:T(8,128)S(1)} fusion(f32[512,6,768]{2,1,0:T(8,128)} %reshape.147, f32[512,6]{1,0:T(8,128)S(1)} %copy.40), kind=kLoop, calls=%fused_computation.5 | loop fusion | flops 4325376 | bytes 11022336 | tf_op jit(solution)/shard_map/reduce_sum | solution.py:116
  375.5 2.7 add_convert_fusion
  (64 shorter events, 9.2 us)
Async XLA Ops:
  6.5 169.8 %copy-start = (bf16[1,768,1024]{2,1,0:T(8,128)(2,1)S(1)}, bf16[1,768,1024]{2,1,0:T(8,128)(2,1)}, u32[]{:S(2)}) copy-start(bf16[1,768,1024]{2,1,0:T(8,128)(2,1)} %param.17) | copy-start | bytes 4718596
  6.5 196.7 %reduce-scatter.5.cloned.1.call-start = ((), (), s32[]{:S(2)}) async-start(), calls=%async_computation.6 | async-start | bytes 10223616 | tf_op jit(solution)/shard_map/reduce_scatter | solution.py:93
  9.5 49.6 %copy-start.2 = (bf16[512,768]{1,0:T(8,128)(2,1)S(1)}, bf16[512,768]{1,0:T(8,128)(2,1)}, u32[]{:S(2)}) copy-start(bf16[512,768]{1,0:T(8,128)(2,1)} %param.11) | copy-start | bytes 2359300
  186.3 38.8 %all-gather.5.cloned.1.call-start = ((), (), s32[]{:S(2)}) async-start(), calls=%async_computation.7 | async-start | bytes 5111808 | tf_op jit(solution)/shard_map/all_gather | solution.py:103
  206.0 19.1 %copy-start.9 = (bf16[1,512,768]{2,1,0:T(8,128)(2,1)S(1)}, bf16[1,512,768]{2,1,0:T(8,128)(2,1)}, u32[]{:S(2)}) copy-start(bf16[1,512,768]{2,1,0:T(8,128)(2,1)} %param.18) | copy-start | bytes 2359300
  239.6 11.5 %copy-start.3 = (bf16[512,768]{1,0:T(8,128)(2,1)S(1)}, bf16[512,768]{1,0:T(8,128)(2,1)}, u32[]{:S(2)}) copy-start(bf16[512,768]{1,0:T(8,128)(2,1)} %param.11) | copy-start | bytes 2359300
  239.6 11.5 %copy-start.6 = (bf16[768,64]{0,1:T(8,128)(2,1)S(1)}, bf16[768,64]{0,1:T(8,128)(2,1)}, u32[]{:S(2)}) copy-start(bf16[768,64]{0,1:T(8,128)(2,1)} %param.12) | copy-start | bytes 294916
  239.6 12.5 %copy-start.5 = (bf16[768,256]{1,0:T(8,128)(2,1)S(1)}, bf16[768,256]{1,0:T(8,128)(2,1)}, u32[]{:S(2)}) copy-start(bf16[768,256]{1,0:T(8,128)(2,1)} %param.13) | copy-start | bytes 1179652
  239.6 84.4 %all-to-all-start.1 = ((bf16[64,52,768]{2,1,0:T(8,128)(2,1)}), bf16[64,52,768]{2,1,0:T(8,128)(2,1)}, u32[]{:S(2)}, u32[]{:S(2)}) async-start(bf16[64,52,768]{2,1,0:T(8,128)(2,1)} %reshape.144), calls=%async_computation.3 | async-start | bytes 11010048 | tf_op jit(solution)/shard_map/all_to_all | solution.py:107
  250.3 16.3 %all-gather.3.cloned.1.call-start = ((), (), s32[]{:S(2)}) async-start(), calls=%async_computation.4 | async-start | bytes 2359296 | tf_op jit(solution)/shard_map/all_gather | solution.py:59
  251.0 43.3 %all-reduce.3.cloned.1.call-start = ((), (), s32[]{:S(2)}) async-start(), calls=%async_computation.8 | async-start | bytes 655360 | tf_op jit(solution)/shard_map/psum | solution.py:41
  253.2 122.3 %reduce-scatter.3.cloned.1.call-start = ((), (), s32[]{:S(2)}) async-start(), calls=%async_computation.5 | async-start | bytes 2359296 | tf_op jit(solution)/shard_map/reduce_scatter | solution.py:67
  266.6 4.3 %copy-start.8 = (bf16[512,1536]{1,0:T(8,128)(2,1)S(1)}, bf16[512,1536]{1,0:T(8,128)(2,1)}, u32[]{:S(2)}) copy-start(bf16[512,1536]{1,0:T(8,128)(2,1)} %param.16) | copy-start | bytes 4718596
  270.9 2.3 copy-start.4
  270.9 2.6 copy-start.10
  270.9 2.9 copy-start.7
  358.2 19.9 %copy-start.1 = (bf16[1,768,1024]{2,1,0:T(8,128)(2,1)S(1)}, bf16[1,768,1024]{2,1,0:T(8,128)(2,1)}, u32[]{:S(2)}) copy-start(bf16[1,768,1024]{2,1,0:T(8,128)(2,1)} %param.17) | copy-start | bytes 4718596
Sparse Core Ops, SparseCore 0:
  186.4 16.7 reduce-scatter.4
  208.5 16.5 all-gather.4
  252.8 13.7 all-gather.2
  268.9 25.3 all-reduce.2
  296.5 13.0 reduce-scatter.2
where the time goes:
time: 388 us; the launch traced here: 385 us
  local copies, waits for them, and re-layouts  126 us (32%)
  blocking collectives  76 us (20%)
  waiting for transfers between devices  66.6 us (17%)
  other arithmetic  63.6 us (16%)
  matrix products  28.2 us (7%)
  between operations  13.4 us (3%)
  starting transfers between devices  11.3 us (3%)
    all_to_all x1, blocking collectives, body(): lax.all_to_all(send_rows.reshape(expert_count, most_rows, feat_local), 'r...  76 us
    another operation x4, other arithmetic  33.5 us
    gather x5, local copies, waits for them, and re-layouts, body(): chosen = jnp.take_along_axis(scores, routes, axis=1)  25.5 us
    psum x1, waiting for transfers between devices, body(): lax.psum(logit_part.astype(jnp.bfloat16), 'blk').astype(jnp.float32)  20.4 us
    gather x2, local copies, waits for them, and re-layouts, body(): normed[source_slot]  18.2 us
    gather x1, local copies, waits for them, and re-layouts, body(): returned.reshape(expert_count * most_rows, feat_local)[target]  17.7 us
    reduce_sum x1, other arithmetic, body(): routed = jnp.sum(weighted.reshape(tok_rows, top_count, feat_local), axis=1)  17.2 us
    reduce_scatter x1, waiting for transfers between devices, body(): lax.psum_scatter(jnp.dot(rows_in, weight_gate_up, preferred_element_type=...  16.7 us
  transfers between devices with their start and end apart: 6, of which 5 were waited for; matrix products, arithmetic and copies ran while one was open for 24% of the time, Pallas kernels for 0%

commit v1 on v0

--- a/solution.py
+++ b/solution.py
@@ -56,7 +56,15 @@
     shared_local = shared_gate_up.shape[2]
     shared_flat = shared_gate_up.reshape(shared_gate_up.shape[0], 2 * shared_local)
     shared_pre = jnp.dot(
-        lax.all_gather(normed, "blk", axis=1, tiled=True),
+        jnp.concatenate(
+            jax.lax.all_to_all(
+                jnp.stack([normed for _ in range(jax.lax.axis_size("blk"))]),
+                axis_name="blk",
+                split_axis=0,
+                concat_axis=0,
+            ),
+            axis=1,
+        ),
         shared_flat,
         preferred_element_type=jnp.float32,
     )

time: 388 us -> 372 us (0.959)
  other arithmetic: 63.6 us -> 50.4 us
    all_to_all x1, waiting for transfers between devices: 3.31 us -> 18.6 us  [body(): lax.all_to_all(expert_out.reshape(req_count, most_rows, feat_local), 'req...]
    another operation x4 -> x5, other arithmetic: 33.5 us -> 21.2 us
    all_gather x1 -> x0, waiting for transfers between devices: 8.64 us -> none  [body(): lax.all_gather(normed, 'blk', axis=1, tiled=True)]
    all_gather x1, waiting for transfers between devices: 16.7 us -> 11.3 us  [body(): lax.all_gather(hidden, 'blk', axis=0, tiled=True)]
  transfers between devices with their start and end apart: 6 -> 6, of which waited for: 5 -> 4; matrix products, arithmetic and copies ran while one was open for 24% -> 28% of each run, Pallas kernels for 0% -> 0%
where the time goes in v1:
time: 372 us; the launch traced here: 370 us
  local copies, waits for them, and re-layouts  124 us (33%)
  blocking collectives  76 us (20%)
  waiting for transfers between devices  65.7 us (18%)
  other arithmetic  50.4 us (14%)
  matrix products  26 us (7%)
  starting transfers between devices  14.7 us (4%)
  between operations  13.4 us (4%)
    all_to_all x1, blocking collectives, body(): lax.all_to_all(send_rows.reshape(expert_count, most_rows, feat_local), 'r...  76 us
    gather x5, local copies, waits for them, and re-layouts, body(): chosen = jnp.take_along_axis(scores, routes, axis=1)  25.5 us
    another operation x4, other arithmetic  19.9 us
    psum x1, waiting for transfers between devices, body(): lax.psum(logit_part.astype(jnp.bfloat16), 'blk').astype(jnp.float32)  18.8 us
    all_to_all x1, waiting for transfers between devices, body(): lax.all_to_all(expert_out.reshape(req_count, most_rows, feat_local), 'req...  18.6 us
    gather x2, local copies, waits for them, and re-layouts, body(): normed[source_slot]  18.2 us
    gather x1, local copies, waits for them, and re-layouts, body(): returned.reshape(expert_count * most_rows, feat_local)[target]  17.7 us
    reduce_sum x1, other arithmetic, body(): routed = jnp.sum(weighted.reshape(tok_rows, top_count, feat_local), axis=1)  17.2 us
  transfers between devices with their start and end apart: 6, of which 4 were waited for; matrix products, arithmetic and copies ran while one was open for 28% of the time, Pallas kernels for 0%

profile of v1, /device:TPU:10, one launch (start us, length us, event | category | flops | bytes accessed | tf_op | source)
XLA Modules:
  0.0 370.3 jit_solution(4332792420401776363)
XLA Ops:
  8.7 18.3 %reduce-window.19 = s32[64,24,128]{2,1,0:T(8,128)S(1)} reduce-window(s32[64,24,128]{2,1,0:T(8,128)S(1)} %fusion.7, s32[]{:T(128)} %constant.58.clone.1), window={size=1x1x128 pad=0_0x0_0x127_0}, to_apply=%region_5.6 | reduce-window | flops 24969216 | bytes 1572868 | tf_op jit(solution)/shard_map/reduce-window.1
  28.2 1.6 copy.44
  29.9 1.2 broadcast_add_fusion
  31.4 1.3 fusion.5
  32.8 11.8 %scatter_custom_fusion.1 = s32[3328]{0:T(1024)S(1)} fusion(s32[3072]{0:T(1024)S(1)} %bitcast.58, s32[3072]{0:T(1024)S(1)} %add_select_fusion, s32[]{:T(128)} %constant.58.clone.1), kind=kCustom, calls=%fused_computation.49 | custom fusion | bytes 13316 | tf_op jit(solution)/shard_map/scatter | solution.py:10
  44.6 10.8 %gather_fusion = bf16[3328,768]{1,0:T(8,128)(2,1)} fusion(bf16[512,768]{1,0:T(8,128)(2,1)S(1)} %copy-done.2, s32[4096]{0:T(1024)S(1)} %pad_clamp_fusion), kind=kCustom, calls=%fused_computation | custom fusion | bytes 10236928 | tf_op jit(solution)/shard_map/gather | solution.py:92
  55.5 7.4 %gather.13 = bf16[64,52,768]{2,1,0:T(8,128)(2,1)} reshape(bf16[3328,768]{1,0:T(8,128)(2,1)} %gather_fusion) | data formatting | bytes 10223616 | tf_op jit(solution)/shard_map/gather | solution.py:92
  62.8 11.8 %scatter_custom_fusion = s32[3328]{0:T(1024)S(1)} fusion(s32[3072]{0:T(1024)S(1)} %bitcast.59, s32[3072]{0:T(1024)S(1)} %broadcast.128, s32[]{:T(128)} %constant.58.clone.1), kind=kCustom, calls=%fused_computation.52 | custom fusion | bytes 13316 | tf_op jit(solution)/shard_map/scatter | solution.py:11
  74.7 3.6 broadcast_select_fusion
  78.3 76.0 %all_to_all.15 = bf16[64,52,768]{2,1,0:T(8,128)(2,1)} all-to-all(bf16[64,52,768]{2,1,0:T(8,128)(2,1)S(1)} %broadcast_select_fusion), channel_id=1, replica_groups=mesh['req'=64,'blk'=2] {'req'}, dimensions={0} | all-to-all | bytes 10223616 | tf_op jit(solution)/shard_map/all_to_all | solution.py:93
  154.4 7.4 %reshape.151 = bf16[3328,768]{1,0:T(8,128)(2,1)} reshape(bf16[64,52,768]{2,1,0:T(8,128)(2,1)} %all_to_all.15) | data formatting | bytes 10223616 | tf_op jit(solution)/shard_map/reshape | solution.py:100
  161.8 10.0 %convolution_convert_fusion = bf16[3328,1024]{1,0:T(8,128)(2,1)} fusion(bf16[3328,768]{1,0:T(8,128)(2,1)} %reshape.151, bf16[1,768,1024]{2,1,0:T(8,128)(2,1)S(1)} %copy-done), kind=kOutput, calls=%fused_computation.6 | convolution fusion | flops 5237899264 | bytes 13500416 | tf_op jit(solution)/shard_map/dot_general | solution.py:102
  171.8 16.9 %reduce-scatter.5.cloned.1.call-done = bf16[1664,1024]{1,0:T(8,128)(2,1)} async-done(((bf16[3328,1024]{1,0:T(8,128)(2,1)}), bf16[1664,1024]{1,0:T(8,128)(2,1)}) %reduce-scatter.5.cloned.1.call-update) | async-done | bytes 3407888 | tf_op jit(solution)/shard_map/reduce_scatter | solution.py:101
  188.7 2.8 convert_element_type.66
  191.5 2.4 fusion
  194.2 1.3 pad_maximum_fusion
  195.5 3.9 %all-to-all-start = ((bf16[2,512,768]{1,2,0:T(8,128)(2,1)}), bf16[2,512,768]{1,2,0:T(8,128)(2,1)S(1)}, u32[]{:S(2)}, u32[]{:S(2)}) async-start(bf16[2,512,768]{1,2,0:T(8,128)(2,1)} %pad_maximum_fusion), calls=%async_computation | async-start | bytes 3145728 | tf_op jit(solution)/shard_map/all_to_all | solution.py:60
  199.3 11.3 %all-gather.2.cloned.1.call-done = bf16[3328,512]{1,0:T(8,128)(2,1)} async-done(((bf16[1664,512]{1,0:T(8,128)(2,1)}), bf16[3328,512]{1,0:T(8,128)(2,1)}) %all-gather.2.cloned.1.call-update) | async-done | bytes 3407888 | tf_op jit(solution)/shard_map/all_gather | solution.py:111
  210.6 7.3 %convolution_convert_fusion.1 = bf16[3328,768]{1,0:T(8,128)(2,1)} fusion(bf16[3328,512]{1,0:T(8,128)(2,1)} %all-gather.2.cloned.1.call-done, bf16[1,512,768]{2,1,0:T(8,128)(2,1)} %param.18), kind=kOutput, calls=%fused_computation.7 | convolution fusion | flops 2619801600 | bytes 9306112 | tf_op jit(solution)/shard_map/dot_general | solution.py:110
  217.9 7.4 %reshape.152 = bf16[64,52,768]{2,1,0:T(8,128)(2,1)} reshape(bf16[3328,768]{1,0:T(8,128)(2,1)} %convolution_convert_fusion.1) | data formatting | bytes 10223616 | tf_op jit(solution)/shard_map/reshape | solution.py:116
  225.3 10.7 %all-to-all-start.2 = ((bf16[64,52,768]{2,1,0:T(8,128)(2,1)}), bf16[64,52,768]{2,1,0:T(8,128)(2,1)}, u32[]{:S(2)}, u32[]{:S(2)}) async-start(bf16[64,52,768]{2,1,0:T(8,128)(2,1)} %reshape.152), calls=%async_computation.4 | async-start | bytes 11010048 | tf_op jit(solution)/shard_map/all_to_all | solution.py:115
  238.2 2.7 copy.45
  240.9 1.8 fusion.23
  242.8 2.2 convolution_convert_fusion.2
  245.8 18.8 %all-reduce.3.cloned.1.call-done = (bf16[512,64]{0,1:T(8,128)(2,1)}, bf16[512,256]{1,0:T(8,128)(2,1)}) async-done(((bf16[512,64]{0,1:T(8,128)(2,1)}, bf16[512,256]{1,0:T(8,128)(2,1)}), (bf16[512,64]{0,1:T(8,128)(2,1)}, bf16[512,256]{1,0:T(8,128)(2,1)})) %all-reduce.3.cloned.1.call-update) | async-done | bytes 327696 | tf_op jit(solution)/shard_map/psum | solution.py:41
  265.5 24.9 %gather_fusion.2 = f32[3072]{0:T(1024)S(1)} fusion(f32[512,64]{0,1:T(8,128)S(1)} %add_divide_fusion, s32[3072]{0:T(1024)S(1)} %reshape.172), kind=kCustom, calls=%fused_computation.2 | custom fusion | bytes 49152 | tf_op jit(solution)/shard_map/jit(take_along_axis)/gather | solution.py:79
  290.9 18.6 %all-to-all-done.2 = bf16[64,52,768]{2,1,0:T(8,128)(2,1)} async-done(((bf16[64,52,768]{2,1,0:T(8,128)(2,1)}), bf16[64,52,768]{2,1,0:T(8,128)(2,1)}, u32[]{:S(2)}, u32[]{:S(2)}) %all-to-all-start.2) | async-done | bytes 5111840 | tf_op jit(solution)/shard_map/all_to_all | solution.py:115
  309.6 7.5 %reshape.153 = bf16[3328,768]{1,0:T(8,128)(2,1)} reshape(bf16[64,52,768]{2,1,0:T(8,128)(2,1)} %all-to-all-done.2) | data formatting | bytes 10223616 | tf_op jit(solution)/shard_map/reshape | solution.py:122
  317.0 17.7 %gather_fusion.1 = bf16[3072,768]{1,0:T(8,128)(2,1)} fusion(bf16[3328,768]{1,0:T(8,128)(2,1)} %reshape.153, s32[3072]{0:T(1024)S(1)} %broadcast_clamp_fusion), kind=kCustom, calls=%fused_computation.1 | custom fusion | bytes 9449472 | tf_op jit(solution)/shard_map/gather | solution.py:122
  334.7 9.2 %reshape.155 = f32[512,6,768]{2,1,0:T(8,128)} reshape(bf16[3072,768]{1,0:T(8,128)(2,1)} %gather_fusion.1) | data formatting | bytes 14155776 | tf_op jit(solution)/shard_map/convert_element_type | solution.py:122
  343.9 17.2 %multiply_reduce_fusion = f32[512,768]{1,0:T(8,128)S(1)} fusion(f32[512,6,768]{2,1,0:T(8,128)} %reshape.155, f32[512,6]{1,0:T(8,128)S(1)} %copy.43), kind=kLoop, calls=%fused_computation.5 | loop fusion | flops 4325376 | bytes 11022336 | tf_op jit(solution)/shard_map/reduce_sum | solution.py:124
  361.1 2.7 add_convert_fusion
  (61 shorter events, 8.6 us)
Async XLA Ops:
  6.5 155.2 %copy-start = (bf16[1,768,1024]{2,1,0:T(8,128)(2,1)S(1)}, bf16[1,768,1024]{2,1,0:T(8,128)(2,1)}, u32[]{:S(2)}) copy-start(bf16[1,768,1024]{2,1,0:T(8,128)(2,1)} %param.17) | copy-start | bytes 4718596
  6.5 182.2 %reduce-scatter.5.cloned.1.call-start = ((), (), s32[]{:S(2)}) async-start(), calls=%async_computation.6 | async-start | bytes 10223616 | tf_op jit(solution)/shard_map/reduce_scatter | solution.py:101
  27.0 17.6 %copy-start.2 = (bf16[512,768]{1,0:T(8,128)(2,1)S(1)}, bf16[512,768]{1,0:T(8,128)(2,1)}, u32[]{:S(2)}) copy-start(bf16[512,768]{1,0:T(8,128)(2,1)} %param.11) | copy-start | bytes 2359300
  171.8 38.9 %all-gather.2.cloned.1.call-start = ((), (), s32[]{:S(2)}) async-start(), calls=%async_computation.7 | async-start | bytes 5111808 | tf_op jit(solution)/shard_map/all_gather | solution.py:111
  195.5 29.8 %all-to-all-start = ((bf16[2,512,768]{1,2,0:T(8,128)(2,1)}), bf16[2,512,768]{1,2,0:T(8,128)(2,1)S(1)}, u32[]{:S(2)}, u32[]{:S(2)}) async-start(bf16[2,512,768]{1,2,0:T(8,128)(2,1)} %pad_maximum_fusion), calls=%async_computation | async-start | bytes 3145728 | tf_op jit(solution)/shard_map/all_to_all | solution.py:60
  225.3 10.8 %copy-start.5 = (bf16[768,64]{0,1:T(8,128)(2,1)S(1)}, bf16[768,64]{0,1:T(8,128)(2,1)}, u32[]{:S(2)}) copy-start(bf16[768,64]{0,1:T(8,128)(2,1)} %param.12) | copy-start | bytes 294916
  225.3 11.8 %copy-start.4 = (bf16[768,256]{1,0:T(8,128)(2,1)S(1)}, bf16[768,256]{1,0:T(8,128)(2,1)}, u32[]{:S(2)}) copy-start(bf16[768,256]{1,0:T(8,128)(2,1)} %param.13) | copy-start | bytes 1179652
  225.3 84.3 %all-to-all-start.2 = ((bf16[64,52,768]{2,1,0:T(8,128)(2,1)}), bf16[64,52,768]{2,1,0:T(8,128)(2,1)}, u32[]{:S(2)}, u32[]{:S(2)}) async-start(bf16[64,52,768]{2,1,0:T(8,128)(2,1)} %reshape.152), calls=%async_computation.4 | async-start | bytes 11010048 | tf_op jit(solution)/shard_map/all_to_all | solution.py:115
  236.0 28.6 %all-reduce.3.cloned.1.call-start = ((), (), s32[]{:S(2)}) async-start(), calls=%async_computation.8 | async-start | bytes 655360 | tf_op jit(solution)/shard_map/psum | solution.py:41
  238.1 123.0 %reduce-scatter.3.cloned.1.call-start = ((), (), s32[]{:S(2)}) async-start(), calls=%async_computation.5 | async-start | bytes 2359296 | tf_op jit(solution)/shard_map/reduce_scatter | solution.py:75
  240.9 1.8 copy-start.7
  242.7 2.3 copy-start.3
  242.8 2.6 copy-start.8
  242.8 2.9 copy-start.6
  343.9 19.9 %copy-start.1 = (bf16[1,768,1024]{2,1,0:T(8,128)(2,1)S(1)}, bf16[1,768,1024]{2,1,0:T(8,128)(2,1)}, u32[]{:S(2)}) copy-start(bf16[1,768,1024]{2,1,0:T(8,128)(2,1)} %param.17) | copy-start | bytes 4718596
Sparse Core Ops, SparseCore 0:
  171.9 16.7 reduce-scatter.4
  194.0 16.5 all-gather.1
  239.3 25.2 all-reduce.2
  266.8 13.0 reduce-scatter.2
